TPU v7x, 256 devices: a whole 4x4x8 slice. The times are simulated.
256 devices in a mesh: pair: 128 (over x, z, y), aux: 2 (over core).
Axes of the slice: x: 4, y: 4, z: 8, core: 2. Of those that a mesh axis runs over, the one named last changes fastest.
Arguments:
- amplitudes: bfloat16 [16384, 128, 128], P('pair', 'aux'), may hold values from -6 to 6
- k_term: bfloat16 [16384, 128, 128], P('pair', 'aux'), may hold values from -6 to 6
- margin_table: bfloat16 [1024, 128, 128], P('pair'), may hold values from -0.5 to 0.5
- margin_index: int32 [16384], P('pair'), may hold values from 0 to 7
- factors: bfloat16 [128, 512, 128], P('pair', 'aux'), may hold values from -6 to 6
- vir_energy: float32 [16384, 128], P('pair'), may hold values from 0.5 to 3
- occ_energy: float32 [128], replicated, may hold values from -2 to -0.3
- pair_owner: int32 [16384, 1], P('pair'), may hold values from 0 to 127; in each aligned block of 128 rows (0 to 127, 128 to 255, ...) at most 2 rows name the same one
Outputs:
- updated: bfloat16 [16384, 128, 128], P('pair', 'aux')
Inputs may be any that keep to these rules, and one draw needn't show every extreme that they name: `pair_owner`: no more than 2 of the 128 pairs of one aligned block name the same owner. `margin_index`: an index into the 8 margin blocks that belong to the pair's aligned block of 128 pairs.
All inputs are finite; a program needn't handle non-finite values.
Results may differ from a plain program's by a relative error of at most 0.0055.
Values may be sent and summed in bfloat16 or wider, within the bound.
No kernel may reach another device: no remote copies, remote signals or barrier semaphores. Data moves between devices by JAX's collectives and lax.ppermute only.
A program may use at most 128 MiB of HBM per device.

v0:
```python
import jax
import jax.numpy as jnp
from jax import lax
from jax.sharding import PartitionSpec as P


def local(
    amplitudes, k_term, margin_table, margin_index, factors, vir_energy, occ_energy, pair_owner
):
    axis_pairs = lax.axis_size("pair")
    aux_count = lax.axis_size("aux")
    own_index = lax.axis_index("pair")
    aux_index = lax.axis_index("aux")
    pair_count = amplitudes.shape[0]
    row_count = amplitudes.shape[1]
    vir_width = amplitudes.shape[2]
    aux_rows = factors.shape[1]
    ovl_count = margin_table.shape[0]
    cycle_scale = float(vir_width * aux_rows * aux_count * pair_count) ** (-0.5)
    every_factor = lax.all_gather(factors[0], ("pair", "aux"), axis=0, tiled=True)
    every_factor = every_factor.reshape(axis_pairs, aux_count * aux_rows, vir_width)
    own_factors = lax.dynamic_index_in_dim(every_factor, own_index, 0, keepdims=False)
    full_amp = lax.all_gather(amplitudes, "aux", axis=1, tiled=True)
    block_pick = (margin_index[:, None] == jnp.arange(ovl_count, dtype=jnp.int32)[None, :]).astype(
        jnp.bfloat16
    )
    margin = jnp.einsum(
        "po,oab->pab", block_pick, margin_table, preferred_element_type=jnp.float32
    ).astype(jnp.bfloat16)
    halfway = jnp.einsum(
        "pca,pab->pcb", full_amp, margin, preferred_element_type=jnp.float32
    ).astype(jnp.bfloat16)
    rotated = jnp.einsum(
        "pac,pab->pcb", margin, halfway, preferred_element_type=jnp.float32
    ).astype(jnp.bfloat16)
    rotated = lax.dynamic_slice_in_dim(rotated, aux_index * row_count, row_count, 1)
    pair_dest = pair_owner[:, 0]
    owner_pick = (jnp.arange(axis_pairs, dtype=jnp.int32)[:, None] == pair_dest[None, :]).astype(
        jnp.bfloat16
    )
    outgoing = jnp.einsum(
        "jp,pcb->jcb", owner_pick, rotated, preferred_element_type=jnp.float32
    ).astype(jnp.bfloat16)
    incoming = lax.all_to_all(outgoing, "pair", 0, 0, tiled=True)
    dressed = jnp.einsum(
        "ica,iqa->cq", incoming, every_factor, preferred_element_type=jnp.float32
    ).astype(jnp.bfloat16)
    local_cycle = jnp.dot(dressed, own_factors, preferred_element_type=jnp.float32)
    cycle_vals = (cycle_scale * local_cycle).astype(jnp.bfloat16)
    slot_back = jnp.broadcast_to(cycle_vals[None], (axis_pairs, row_count, vir_width))
    returned = lax.all_to_all(slot_back, "pair", 0, 0, tiled=True)
    own_cycle = jnp.einsum(
        "jp,jca->pca", owner_pick, returned, preferred_element_type=jnp.float32
    ).astype(jnp.bfloat16)
    cycle_term = jnp.einsum("pca,pba->pcb", own_cycle, margin, preferred_element_type=jnp.float32)
    occ_sum = occ_energy[own_index] + occ_energy[pair_dest]
    energy_rows = lax.dynamic_slice_in_dim(vir_energy, aux_index * row_count, row_count, 1)
    denominator = energy_rows[:, :, None] + vir_energy[:, None, :] - occ_sum[:, None, None]
    updated = (
        amplitudes.astype(jnp.float32) - (cycle_term + k_term.astype(jnp.float32)) / denominator
    )
    return updated.astype(jnp.bfloat16)


def solution(mesh):
    placed = (
        P("pair", "aux", None),
        P("pair", "aux", None),
        P("pair", None, None),
        P("pair"),
        P("pair", "aux", None),
        P("pair", None),
        P(),
        P("pair", None),
    )
    return jax.shard_map(
        local, mesh=mesh, in_specs=placed, out_specs=P("pair", "aux", None), check_vma=False
    )
```

profile of v0, /device:TPU:32, one launch (start us, length us, event | category | flops | bytes accessed | tf_op | source)
XLA Modules:
  0.0 267.1 jit_solution(3907826029855658009)
XLA Ops:
  6.5 0.0 copy-start
  6.5 0.0 all-gather.4.cloned.1.call-start
  6.5 0.7 all-gather.4.cloned.1.call-update
  7.3 0.0 all-gather.6.cloned.1.call-start
  7.3 0.7 all-gather.6.cloned.1.call-update
  8.0 0.0 copy-done
  8.0 3.9 %convolution_convert_fusion = bf16[128,128,128]{2,0,1:T(8,128)(2,1)} fusion(bf16[8,128,128]{2,1,0:T(8,128)(2,1)S(1)} %copy-done, s32[128]{0:T(128)} %param.11), kind=kOutput, calls=%fused_computation.11 | convolution fusion | flops 35652608 | bytes 4456960 | tf_op jit(solution)/shard_map/po,oab->pab/dot_general | solution.py:27
  11.9 18.9 %all-gather.4.cloned.1.call-done = bf16[128,128,128]{2,1,0:T(8,128)(2,1)} async-done(((bf16[128,64,128]{2,1,0:T(8,128)(2,1)}), bf16[128,128,128]{2,1,0:T(8,128)(2,1)}) %all-gather.4.cloned.1.call-update) | async-done | bytes 4194320 | tf_op jit(solution)/shard_map/all_gather | solution.py:23
  30.8 13.0 %fusion = bf16[128,128,128]{2,1,0:T(8,128)(2,1)} fusion(bf16[128,128,128]{2,1,0:T(8,128)(2,1)} %all-gather.4.cloned.1.call-done, bf16[128,128,128]{2,0,1:T(8,128)(2,1)} %convolution_convert_fusion), kind=kOutput, calls=%fused_computation.5 | convolution fusion | flops 1075838976 | bytes 12582912 | tf_op jit(solution)/shard_map/pac,pab->pcb/dot_general | solution.py:33
  43.8 0.0 copy-start.4
  43.8 1.8 dynamic-slice_convert_fusion
  45.6 0.0 copy-done.4
  45.6 1.8 fusion.10
  47.4 2.7 %copy.36 = bf16[128,64,128]{2,1,0:T(8,128)(2,1)} copy(bf16[128,64,128]{2,0,1:T(8,128)(2,1)S(1)} %fusion.10) | data formatting | bytes 4194304 | tf_op jit(solution)/shard_map/jp,pcb->jcb/dot_general | solution.py:41
  50.0 13.7 %all-to-all-start = ((bf16[128,64,128]{2,1,0:T(8,128)(2,1)}), bf16[128,64,128]{2,1,0:T(8,128)(2,1)S(1)}, u32[]{:S(2)}, u32[]{:S(2)}) async-start(bf16[128,64,128]{2,1,0:T(8,128)(2,1)} %copy.36), calls=%async_computation | async-start | bytes 4194304 | tf_op jit(solution)/shard_map/all_to_all | solution.py:44
  63.7 59.4 %all-to-all-done = bf16[128,64,128]{2,1,0:T(8,128)(2,1)S(1)} async-done(((bf16[128,64,128]{2,1,0:T(8,128)(2,1)}), bf16[128,64,128]{2,1,0:T(8,128)(2,1)S(1)}, u32[]{:S(2)}, u32[]{:S(2)}) %all-to-all-start) | async-done | bytes 2097184 | tf_op jit(solution)/shard_map/all_to_all | solution.py:44
  123.1 43.7 %all-gather.6.cloned.1.call-done = bf16[1,65536,128]{2,1,0:T(8,128)(2,1)} async-done(((bf16[1,256,128]{2,1,0:T(8,128)(2,1)}), bf16[1,65536,128]{2,1,0:T(8,128)(2,1)}) %all-gather.6.cloned.1.call-update) | async-done | bytes 16777232 | tf_op jit(solution)/shard_map/all_gather | solution.py:20
  166.8 11.0 %fusion.15 = bf16[64,128]{1,0:T(8,128)(2,1)S(1)} fusion(bf16[128,64,128]{2,1,0:T(8,128)(2,1)S(1)} %all-to-all-done, bf16[128,512,128]{2,1,0:T(8,128)(2,1)} %bitcast.24, s32[]{:T(128)S(6)} %select_n.14), kind=kOutput, calls=%fused_computation.19 | convolution fusion | flops 1082179584 | bytes 19021828 | tf_op jit(solution)/shard_map/dot_general | solution.py:48
  177.8 0.0 copy-start.1
  177.9 0.0 copy-start.3
  177.9 1.8 broadcast_in_dim.2
  179.7 9.7 %all-to-all-start.1 = ((bf16[128,64,128]{2,1,0:T(8,128)(2,1)}), bf16[128,64,128]{2,1,0:T(8,128)(2,1)S(1)}, u32[]{:S(2)}, u32[]{:S(2)}) async-start(bf16[128,64,128]{2,1,0:T(8,128)(2,1)} %broadcast_in_dim.2), calls=%async_computation.1 | async-start | bytes 4194304 | tf_op jit(solution)/shard_map/all_to_all | solution.py:51
  189.5 0.0 copy-done.1
  189.5 0.6 dynamic_slice.16
  190.1 1.2 gather_fusion
  191.3 0.0 copy-done.3
  191.3 0.1 constant_dynamic-slice_fusion
  191.4 0.6 broadcast_add_fusion
  192.1 50.2 %all-to-all-done.1 = bf16[128,64,128]{2,1,0:T(8,128)(2,1)S(1)} async-done(((bf16[128,64,128]{2,1,0:T(8,128)(2,1)}), bf16[128,64,128]{2,1,0:T(8,128)(2,1)S(1)}, u32[]{:S(2)}, u32[]{:S(2)}) %all-to-all-start.1) | async-done | bytes 2097184 | tf_op jit(solution)/shard_map/all_to_all | solution.py:51
  242.3 0.0 copy-start.2
  242.3 1.8 fusion.8
  244.0 0.4 copy-done.2
  244.5 15.8 %subtract_convert_fusion = bf16[128,64,128]{2,1,0:T(8,128)(2,1)} fusion(bf16[128,64,128]{2,1,0:T(8,128)(2,1)} %param.9, bf16[128,64,128]{2,1,0:T(8,128)(2,1)} %param.8, f32[128]{0:T(128)S(1)} %broadcast_add_fusion, f32[128,128]{1,0:T(8,128)S(1)} %copy-done.3, f32[128,64]{1,0:T(8,128)S(1)} %constant_dynamic-slice_fusion, ...), kind=kOutput, calls=%fused_computation.4 | convolution fusion | flops 276824064 | bytes 12681728 | tf_op jit(solution)/shard_map/pca,pba->pcb/dot_general | solution.py:55
  (2 shorter events, 0.0 us)
Async XLA Ops:
  6.5 1.5 copy-start
  6.5 24.2 %all-gather.4.cloned.1.call-start = ((), (), s32[]{:S(2)}) async-start(), calls=%async_computation.2 | async-start | bytes 6291456 | tf_op jit(solution)/shard_map/all_gather | solution.py:23
  7.3 159.6 %all-gather.6.cloned.1.call-start = ((), (), s32[]{:S(2)}) async-start(), calls=%async_computation.3 | async-start | bytes 16842752 | tf_op jit(solution)/shard_map/all_gather | solution.py:20
  43.8 1.8 copy-start.4
  50.0 73.1 %all-to-all-start = ((bf16[128,64,128]{2,1,0:T(8,128)(2,1)}), bf16[128,64,128]{2,1,0:T(8,128)(2,1)S(1)}, u32[]{:S(2)}, u32[]{:S(2)}) async-start(bf16[128,64,128]{2,1,0:T(8,128)(2,1)} %copy.36), calls=%async_computation | async-start | bytes 4194304 | tf_op jit(solution)/shard_map/all_to_all | solution.py:44
  177.8 11.6 %copy-start.1 = (f32[128]{0:T(128)S(1)}, f32[128]{0:T(128)}, u32[]{:S(2)}) copy-start(f32[128]{0:T(128)} %param.14) | copy-start | bytes 1540
  177.9 13.5 %copy-start.3 = (f32[128,128]{1,0:T(8,128)S(1)}, f32[128,128]{1,0:T(8,128)}, u32[]{:S(2)}) copy-start(f32[128,128]{1,0:T(8,128)} %param.13) | copy-start | bytes 196612
  179.7 62.6 %all-to-all-start.1 = ((bf16[128,64,128]{2,1,0:T(8,128)(2,1)}), bf16[128,64,128]{2,1,0:T(8,128)(2,1)S(1)}, u32[]{:S(2)}, u32[]{:S(2)}) async-start(bf16[128,64,128]{2,1,0:T(8,128)(2,1)} %broadcast_in_dim.2), calls=%async_computation.1 | async-start | bytes 4194304 | tf_op jit(solution)/shard_map/all_to_all | solution.py:51
  242.3 2.2 copy-start.2
Sparse Core Ops, SparseCore 0:
  9.1 21.6 all-gather.3
  34.5 132.2 all-gather.5
where the time goes:
time: 267 us
  waiting for transfers between devices  174 us (65%)
  matrix products  47.2 us (18%)
  starting transfers between devices  23.5 us (9%)
  between operations  13.5 us (5%)
  local copies, waits for them, and re-layouts  8.68 us (3%)
    all_to_all x1, waiting for transfers between devices, local(): incoming = lax.all_to_all(outgoing, 'pair', 0, 0, tiled=True)  59.4 us
    all_to_all x1, waiting for transfers between devices, local(): returned = lax.all_to_all(slot_back, 'pair', 0, 0, tiled=True)  50.2 us
    all_gather x1, waiting for transfers between devices, local(): lax.all_gather(factors[0], ('pair', 'aux'), axis=0, tiled=True)  43.7 us
    all_gather x1, waiting for transfers between devices, local(): full_amp = lax.all_gather(amplitudes, 'aux', axis=1, tiled=True)  18.9 us
    dot_general x1, matrix products, local(): jnp.einsum('pca,pba->pcb', own_cycle, margin, preferred_element_type=jnp....  15.8 us
    all_to_all x1, starting transfers between devices, local(): incoming = lax.all_to_all(outgoing, 'pair', 0, 0, tiled=True)  13.7 us
    dot_general x1, matrix products, local(): jnp.einsum('pac,pab->pcb', margin, halfway, preferred_element_type=jnp.fl...  13 us
    dot_general x1, matrix products, local(): jnp.dot(dressed, own_factors, preferred_element_type=jnp.float32)  11 us
  transfers between devices with their start and end apart: 4, of which 4 were waited for; matrix products, arithmetic and copies ran while one was open for 10% of the time, Pallas kernels for 0%

commit v1 on v0

--- a/solution.py
+++ b/solution.py
@@ -20,7 +20,9 @@
     every_factor = lax.all_gather(factors[0], ("pair", "aux"), axis=0, tiled=True)
     every_factor = every_factor.reshape(axis_pairs, aux_count * aux_rows, vir_width)
     own_factors = lax.dynamic_index_in_dim(every_factor, own_index, 0, keepdims=False)
-    full_amp = lax.all_gather(amplitudes, "aux", axis=1, tiled=True)
+    full_amp = jnp.concatenate(
+        lax.all_to_all(jnp.stack([amplitudes] * lax.axis_size("aux")), "aux", 0, 0), axis=1
+    )
     block_pick = (margin_index[:, None] == jnp.arange(ovl_count, dtype=jnp.int32)[None, :]).astype(
         jnp.bfloat16
     )

time: 267 us -> 252 us (0.944)
  waiting for transfers between devices: 174 us -> 138 us
  starting transfers between devices: 23.5 us -> 32.4 us
  local copies, waits for them, and re-layouts: 8.68 us -> 14.4 us
  other arithmetic: 0.65 us -> 5.23 us
    all_gather x1, waiting for transfers between devices: 43.7 us -> 18.1 us  [local(): lax.all_gather(factors[0], ('pair', 'aux'), axis=0, tiled=True)]
    all_gather x1 -> x0, waiting for transfers between devices: 18.9 us -> none  [local(): full_amp = lax.all_gather(amplitudes, 'aux', axis=1, tiled=True)]
    all_to_all x0 -> x1, starting transfers between devices: none -> 5.6 us  [local(): lax.all_to_all(jnp.stack([amplitudes] * lax.axis_size('aux')), 'aux', 0, 0)]
    all_to_all x0 -> x1, local copies, waits for them, and re-layouts: none -> 5.56 us  [local(): lax.all_to_all(jnp.stack([amplitudes] * lax.axis_size('aux')), 'aux', 0, 0)]
    all_to_all x1, waiting for transfers between devices: 59.4 us -> 64.6 us  [local(): incoming = lax.all_to_all(outgoing, 'pair', 0, 0, tiled=True)]
    another operation x0 -> x1, other arithmetic: none -> 4.58 us  [local(): jnp.stack([amplitudes] * lax.axis_size('aux'))]
    all_to_all x0 -> x1, waiting for transfers between devices: none -> 4.46 us  [local(): lax.all_to_all(jnp.stack([amplitudes] * lax.axis_size('aux')), 'aux', 0, 0)]
    convert_element_type x0 -> x1, local copies, waits for them, and re-layouts: none -> 2.85 us  [local(): outgoing = jnp.einsum('jp,pcb->jcb', owner_pick, rotated, preferred_eleme...]
  transfers between devices with their start and end apart: 4 -> 4, of which waited for: 4 -> 4; matrix products, arithmetic and copies ran while one was open for 10% -> 15% of each run, Pallas kernels for 0% -> 0%
where the time goes in v1:
time: 252 us; the launch traced here: 251 us
  waiting for transfers between devices  138 us (55%)
  matrix products  47.7 us (19%)
  starting transfers between devices  32.4 us (13%)
  local copies, waits for them, and re-layouts  14.4 us (6%)
  between operations  13.5 us (5%)
  other arithmetic  5.23 us (2%)
    all_to_all x1, waiting for transfers between devices, local(): incoming = lax.all_to_all(outgoing, 'pair', 0, 0, tiled=True)  64.6 us
    all_to_all x1, waiting for transfers between devices, local(): returned = lax.all_to_all(slot_back, 'pair', 0, 0, tiled=True)  50.2 us
    all_gather x1, waiting for transfers between devices, local(): lax.all_gather(factors[0], ('pair', 'aux'), axis=0, tiled=True)  18.1 us
    dot_general x1, matrix products, local(): jnp.einsum('pca,pba->pcb', own_cycle, margin, preferred_element_type=jnp....  15.8 us
    all_to_all x1, starting transfers between devices, local(): incoming = lax.all_to_all(outgoing, 'pair', 0, 0, tiled=True)  15 us
    dot_general x1, matrix products, local(): jnp.einsum('pac,pab->pcb', margin, halfway, preferred_element_type=jnp.fl...  14.1 us
    all_to_all x1, starting transfers between devices, local(): returned = lax.all_to_all(slot_back, 'pair', 0, 0, tiled=True)  11.8 us
    dot_general x1, matrix products, local(): jnp.dot(dressed, own_factors, preferred_element_type=jnp.float32)  11 us
  transfers between devices with their start and end apart: 4, of which 4 were waited for; matrix products, arithmetic and copies ran while one was open for 15% of the time, Pallas kernels for 0%

profile of v1, /device:TPU:32, one launch (start us, length us, event | category | flops | bytes accessed | tf_op | source)
XLA Modules:
  0.0 251.4 jit_solution(7913688990970154867)
XLA Ops:
  6.5 0.0 copy-start
  6.5 0.0 all-gather.3.cloned.1.call-start
  6.5 0.7 all-gather.3.cloned.1.call-update
  7.3 4.6 %pad_maximum_fusion = bf16[2,128,64,128]{3,2,1,0:T(8,128)(2,1)} fusion(bf16[1,128,64,128]{3,2,1,0:T(8,128)(2,1)} %bitcast.31), kind=kLoop, calls=%fused_computation.2 | loop fusion | flops 2097152 | bytes 6291456 | tf_op jit(solution)/shard_map/stack | solution.py:24
  11.8 5.6 %all-to-all-start = ((bf16[2,128,64,128]{3,2,1,0:T(8,128)(2,1)}), bf16[2,128,64,128]{3,2,1,0:T(8,128)(2,1)}, u32[]{:S(2)}, u32[]{:S(2)}) async-start(bf16[2,128,64,128]{3,2,1,0:T(8,128)(2,1)} %pad_maximum_fusion), calls=%async_computation | async-start | bytes 8388608 | tf_op jit(solution)/shard_map/all_to_all | solution.py:24
  17.5 0.0 copy-start.5
  17.5 4.5 %all-to-all-done = bf16[2,128,64,128]{3,2,1,0:T(8,128)(2,1)} async-done(((bf16[2,128,64,128]{3,2,1,0:T(8,128)(2,1)}), bf16[2,128,64,128]{3,2,1,0:T(8,128)(2,1)}, u32[]{:S(2)}, u32[]{:S(2)}) %all-to-all-start) | async-done | bytes 4194336 | tf_op jit(solution)/shard_map/all_to_all | solution.py:24
  21.9 5.6 %copy.23 = bf16[2,128,64,128]{3,2,0,1:T(8,128)(2,1)} copy(bf16[2,128,64,128]{3,2,1,0:T(8,128)(2,1)} %all-to-all-done) | data formatting | bytes 8388608 | tf_op jit(solution)/shard_map/all_to_all | solution.py:24
  27.5 0.0 copy-done
  27.5 0.0 copy-done.5
  27.5 3.2 %convolution_convert_fusion = bf16[128,128,128]{2,0,1:T(8,128)(2,1)} fusion(bf16[8,128,128]{2,1,0:T(8,128)(2,1)S(1)} %copy-done, s32[128]{0:T(128)S(1)} %copy-done.5), kind=kOutput, calls=%fused_computation.10 | convolution fusion | flops 35652608 | bytes 4456960 | tf_op jit(solution)/shard_map/po,oab->pab/dot_general | solution.py:29
  30.7 14.1 %fusion = bf16[128,128,128]{2,1,0:T(8,128)(2,1)} fusion(bf16[128,128,128]{2,1,0:T(8,128)(2,1)} %bitcast.30, bf16[128,128,128]{2,0,1:T(8,128)(2,1)} %convolution_convert_fusion), kind=kOutput, calls=%fused_computation.4 | convolution fusion | flops 1075838976 | bytes 12582912 | tf_op jit(solution)/shard_map/pac,pab->pcb/dot_general | solution.py:35
  44.9 0.0 copy-start.4
  44.9 1.8 dynamic-slice_convert_fusion
  46.7 0.0 copy-done.4
  46.7 1.8 fusion.13
  48.5 2.9 %copy.28 = bf16[128,64,128]{2,1,0:T(8,128)(2,1)} copy(bf16[128,64,128]{2,0,1:T(8,128)(2,1)S(1)} %fusion.13) | data formatting | bytes 4194304 | tf_op jit(solution)/shard_map/convert_element_type | solution.py:45
  51.3 15.0 %all-to-all-start.1 = ((bf16[128,64,128]{2,1,0:T(8,128)(2,1)}), bf16[128,64,128]{2,1,0:T(8,128)(2,1)S(1)}, u32[]{:S(2)}, u32[]{:S(2)}) async-start(bf16[128,64,128]{2,1,0:T(8,128)(2,1)} %copy.28), calls=%async_computation.1 | async-start | bytes 4194304 | tf_op jit(solution)/shard_map/all_to_all | solution.py:46
  66.3 64.6 %all-to-all-done.1 = bf16[128,64,128]{2,1,0:T(8,128)(2,1)S(1)} async-done(((bf16[128,64,128]{2,1,0:T(8,128)(2,1)}), bf16[128,64,128]{2,1,0:T(8,128)(2,1)S(1)}, u32[]{:S(2)}, u32[]{:S(2)}) %all-to-all-start.1) | async-done | bytes 2097184 | tf_op jit(solution)/shard_map/all_to_all | solution.py:46
  130.9 18.1 %all-gather.3.cloned.1.call-done = bf16[1,65536,128]{2,1,0:T(8,128)(2,1)} async-done(((bf16[1,256,128]{2,1,0:T(8,128)(2,1)}), bf16[1,65536,128]{2,1,0:T(8,128)(2,1)}) %all-gather.3.cloned.1.call-update) | async-done | bytes 16777232 | tf_op jit(solution)/shard_map/all_gather | solution.py:20
  149.0 11.0 %fusion.24 = bf16[64,128]{1,0:T(8,128)(2,1)S(1)} fusion(bf16[128,64,128]{2,1,0:T(8,128)(2,1)S(1)} %all-to-all-done.1, bf16[128,512,128]{2,1,0:T(8,128)(2,1)} %bitcast.29, s32[]{:T(128)S(6)} %select_n.14), kind=kOutput, calls=%fused_computation.21 | convolution fusion | flops 1082179584 | bytes 19021828 | tf_op jit(solution)/shard_map/dot_general | solution.py:50
  160.0 0.0 copy-start.1
  160.0 0.0 copy-start.3
  160.1 1.8 broadcast_in_dim.2
  161.9 11.8 %all-to-all-start.2 = ((bf16[128,64,128]{2,1,0:T(8,128)(2,1)}), bf16[128,64,128]{2,1,0:T(8,128)(2,1)S(1)}, u32[]{:S(2)}, u32[]{:S(2)}) async-start(bf16[128,64,128]{2,1,0:T(8,128)(2,1)} %broadcast_in_dim.2), calls=%async_computation.2 | async-start | bytes 4194304 | tf_op jit(solution)/shard_map/all_to_all | solution.py:53
  173.7 0.0 copy-done.1
  173.7 0.6 dynamic_slice.16
  174.4 1.2 gather_fusion
  175.6 0.0 copy-done.3
  175.6 0.1 constant_dynamic-slice_fusion
  175.7 0.6 broadcast_add_fusion
  176.4 50.2 %all-to-all-done.2 = bf16[128,64,128]{2,1,0:T(8,128)(2,1)S(1)} async-done(((bf16[128,64,128]{2,1,0:T(8,128)(2,1)}), bf16[128,64,128]{2,1,0:T(8,128)(2,1)S(1)}, u32[]{:S(2)}, u32[]{:S(2)}) %all-to-all-start.2) | async-done | bytes 2097184 | tf_op jit(solution)/shard_map/all_to_all | solution.py:53
  226.6 0.0 copy-start.2
  226.6 1.7 fusion.16
  228.3 0.4 copy-done.2
  228.7 15.8 %subtract_convert_fusion = bf16[128,64,128]{2,1,0:T(8,128)(2,1)} fusion(bf16[128,64,128]{2,1,0:T(8,128)(2,1)} %param.9, bf16[128,64,128]{2,1,0:T(8,128)(2,1)} %param.8, f32[128]{0:T(128)S(1)} %broadcast_add_fusion, f32[128,128]{1,0:T(8,128)S(1)} %copy-done.3, f32[128,64]{1,0:T(8,128)S(1)} %constant_dynamic-slice_fusion, ...), kind=kOutput, calls=%fused_computation.3 | convolution fusion | flops 276824064 | bytes 12681728 | tf_op jit(solution)/shard_map/pca,pba->pcb/dot_general | solution.py:57
  (2 shorter events, 0.0 us)
Async XLA Ops:
  6.5 21.0 %copy-start = (bf16[8,128,128]{2,1,0:T(8,128)(2,1)S(1)}, bf16[8,128,128]{2,1,0:T(8,128)(2,1)}, u32[]{:S(2)}) copy-start(bf16[8,128,128]{2,1,0:T(8,128)(2,1)} %param.10) | copy-start | bytes 786436
  6.5 142.5 %all-gather.3.cloned.1.call-start = ((), (), s32[]{:S(2)}) async-start(), calls=%async_computation.3 | async-start | bytes 16842752 | tf_op jit(solution)/shard_map/all_gather | solution.py:20
  11.8 10.1 %all-to-all-start = ((bf16[2,128,64,128]{3,2,1,0:T(8,128)(2,1)}), bf16[2,128,64,128]{3,2,1,0:T(8,128)(2,1)}, u32[]{:S(2)}, u32[]{:S(2)}) async-start(bf16[2,128,64,128]{3,2,1,0:T(8,128)(2,1)} %pad_maximum_fusion), calls=%async_computation | async-start | bytes 8388608 | tf_op jit(solution)/shard_map/all_to_all | solution.py:24
  17.5 10.0 %copy-start.5 = (s32[128]{0:T(128)S(1)}, s32[128]{0:T(128)}, u32[]{:S(2)}) copy-start(s32[128]{0:T(128)} %param.11) | copy-start | bytes 1540
  44.9 1.8 copy-start.4
  51.3 79.6 %all-to-all-start.1 = ((bf16[128,64,128]{2,1,0:T(8,128)(2,1)}), bf16[128,64,128]{2,1,0:T(8,128)(2,1)S(1)}, u32[]{:S(2)}, u32[]{:S(2)}) async-start(bf16[128,64,128]{2,1,0:T(8,128)(2,1)} %copy.28), calls=%async_computation.1 | async-start | bytes 4194304 | tf_op jit(solution)/shard_map/all_to_all | solution.py:46
  160.0 13.7 %copy-start.1 = (f32[128]{0:T(128)S(1)}, f32[128]{0:T(128)}, u32[]{:S(2)}) copy-start(f32[128]{0:T(128)} %param.14) | copy-start | bytes 1540
  160.0 15.6 %copy-start.3 = (f32[128,128]{1,0:T(8,128)S(1)}, f32[128,128]{1,0:T(8,128)}, u32[]{:S(2)}) copy-start(f32[128,128]{1,0:T(8,128)} %param.13) | copy-start | bytes 196612
  161.9 64.7 %all-to-all-start.2 = ((bf16[128,64,128]{2,1,0:T(8,128)(2,1)}), bf16[128,64,128]{2,1,0:T(8,128)(2,1)S(1)}, u32[]{:S(2)}, u32[]{:S(2)}) async-start(bf16[128,64,128]{2,1,0:T(8,128)(2,1)} %broadcast_in_dim.2), calls=%async_computation.2 | async-start | bytes 4194304 | tf_op jit(solution)/shard_map/all_to_all | solution.py:53
  226.6 2.2 copy-start.2
Sparse Core Ops, SparseCore 0:
  11.0 137.9 all-gather.2
